TPU v7x, 32 devices: a whole 2x2x4 slice. The times are simulated.
32 devices in a mesh: circ: 4 (over z), normal: 2 (over y), span: 4 (over x, core).
Axes of the slice: x: 2, y: 2, z: 4, core: 2. Of those that a mesh axis runs over, the one named last changes fastest.
Arguments:
- adjoint: float32 [5, 16, 32, 512], P(None, 'span', 'normal', 'circ'), may hold values from -6 to 6
- objective_grad: float32 [5, 16, 32, 512], P(None, 'span', 'normal', 'circ'), may hold values from -6 to 6
- face_weights: float32 [3, 16, 32, 512], P(None, 'span', 'normal', 'circ'), may hold values from 0.2 to 2
- owner_jac: float32 [3, 5, 5], replicated, may hold values from -2.5 to 2.5
- neighbor_jac: float32 [3, 5, 5], replicated, may hold values from -2.5 to 2.5
- coupling: float32 [3, 5], replicated, may hold values from -2.5 to 2.5
- stiffness: float32 [16, 32, 512], P('span', 'normal', 'circ'), may hold values from 0.3 to 3
- wall_kernel: float32 [16, 32, 512], P('span', 'normal', 'circ'), may hold values from -0.25 to 0.25
- panel_owner: int32 [16, 512], P('span', 'circ'), may hold values from 0 to 511, as said below
Outputs:
- adjoint_residual: float32 [5, 16, 32, 512], P(None, 'span', 'normal', 'circ')
- mesh_adjoint: float32 [3, 16, 32, 512], P(None, 'span', 'normal', 'circ')
- panel_sens: float32 [3, 512], P(None, 'span')
Inputs may be any that keep to these rules, and one draw needn't show every extreme that they name: `panel_owner`: the panel of a wall face at station k is owned by span index k // 4 or the one beside it; panels hold ragged numbers of faces.
All inputs are finite; a program needn't handle non-finite values.
Results may differ from a plain program's by a relative error of at most 0.00011.
Values sent between devices are 32-bit elements; how exact they have to be, the bound alone decides.
No kernel may reach another device: no remote copies, remote signals or barrier semaphores. Data moves between devices by JAX's collectives and lax.ppermute only.
A program may use at most 64 MiB of HBM per device.

v0:
```python
import jax
import jax.numpy as jnp
from jax import lax
from jax.sharding import PartitionSpec as P

PANEL_DEV = 128
SWEEPS = 4


def padded_2(array, sides, width, wrap):
    for axis, dim in sides:
        peers, length = (lax.axis_size(axis), array.shape[dim])
        up = [(i, (i + 1) % peers) for i in range(peers if wrap else peers - 1)]
        down = [(j, i) for i, j in up]
        last = lax.slice_in_dim(array, length - width, length, axis=dim)
        initial = lax.slice_in_dim(array, 0, width, axis=dim)
        before = lax.ppermute(last, axis, up)
        after = lax.ppermute(initial, axis, down)
        array = jnp.concatenate([before, array, after], axis=dim)
    return array


def neighbor_sum(padded):
    total = padded[:, 2:, 1:-1, 1:-1] + padded[:, :-2, 1:-1, 1:-1]
    total = total + padded[:, 1:-1, 2:, 1:-1] + padded[:, 1:-1, :-2, 1:-1]
    return total + padded[:, 1:-1, 1:-1, 2:] + padded[:, 1:-1, 1:-1, :-2]


def inner(field):
    return field[:, 1:-1, 1:-1, 1:-1]


def flux_transpose(padded, owner_jac, neighbor_jac):
    psi = padded[:5]
    weights = padded[5:]
    center = inner(psi)
    total = jnp.zeros_like(center)
    for direction in range(3):
        lower = [slice(None), slice(1, -1), slice(1, -1), slice(1, -1)]
        upper = [slice(None), slice(1, -1), slice(1, -1), slice(1, -1)]
        lower[direction + 1] = slice(0, -2)
        upper[direction + 1] = slice(2, None)
        w_here = weights[direction, 1:-1, 1:-1, 1:-1]
        w_lower = weights[direction][tuple(lower[1:])]
        up_term = w_here[None] * (center - psi[tuple(upper)])
        down_term = w_lower[None] * (psi[tuple(lower)] - center)
        total = total + jnp.einsum(
            "uv,ukji->vkji", owner_jac[direction], up_term, precision=lax.Precision.HIGHEST
        )
        total = total + jnp.einsum(
            "uv,ukji->vkji", neighbor_jac[direction], down_term, precision=lax.Precision.HIGHEST
        )
    return total


def relax(mesh_pad, stiff_pad, force_pad):
    weighted = stiff_pad[None] * mesh_pad
    stiff_in = stiff_pad[1:-1, 1:-1, 1:-1]
    diag_term = 6.0 * stiff_in + 1.0
    mesh_in = inner(mesh_pad)
    return (
        mesh_in
        + 0.8
        * (inner(force_pad) - diag_term[None] * mesh_in + neighbor_sum(weighted))
        / diag_term[None]
    )


def run_sweeps(stiff_pad, force_pad):
    mesh_pad = 0.8 * force_pad / (6.0 * stiff_pad[None] + 1.0)
    for sweep in range(1, SWEEPS):
        mesh_pad = relax(mesh_pad, stiff_pad, force_pad)
        stiff_pad = stiff_pad[1:-1, 1:-1, 1:-1]
        force_pad = inner(force_pad)
    return mesh_pad


def on_device(
    adjoint,
    objective_grad,
    face_weights,
    owner_jac,
    neighbor_jac,
    coupling,
    stiffness,
    wall_kernel,
    panel_owner,
):
    stacked = jnp.concatenate([adjoint, face_weights], axis=0)
    beside_all = padded_2(stacked, (("circ", 3),), 1, True)
    padded = padded_2(beside_all, (("normal", 2), ("span", 1)), 1, False)
    residual = flux_transpose(padded, owner_jac, neighbor_jac) + adjoint - objective_grad
    forcing = jnp.einsum("mv,vkji->mkji", coupling, residual, precision=lax.Precision.HIGHEST)
    margin = SWEEPS - 1
    joined = jnp.concatenate([stiffness[None], forcing], axis=0)
    cycle_pad = padded_2(joined, (("circ", 3),), margin, True)
    full_pad = padded_2(cycle_pad, (("normal", 2), ("span", 1)), margin, False)
    mesh = run_sweeps(full_pad[0], full_pad[1:])
    wall_sens = jnp.sum(wall_kernel[None] * mesh, axis=2)
    panel_count = PANEL_DEV * lax.axis_size("span")
    onehot = (
        panel_owner[:, :, None] == jnp.arange(panel_count, dtype=jnp.int32)[None, None, :]
    ).astype(jnp.float32)
    terms = jnp.einsum("mki,kip->mp", wall_sens, onehot, precision=lax.Precision.HIGHEST)
    total = lax.psum(terms, ("circ", "normal", "span"))
    panels = lax.dynamic_slice_in_dim(total, lax.axis_index("span") * PANEL_DEV, PANEL_DEV, 1)
    return (residual, mesh, panels)


def solution(mesh):
    placed = (
        P(None, "span", "normal", "circ"),
        P(None, "span", "normal", "circ"),
        P(None, "span", "normal", "circ"),
        P(),
        P(),
        P(),
        P("span", "normal", "circ"),
        P("span", "normal", "circ"),
        P("span", "circ"),
    )
    return jax.shard_map(
        on_device,
        mesh=mesh,
        in_specs=placed,
        out_specs=(
            P(None, "span", "normal", "circ"),
            P(None, "span", "normal", "circ"),
            P(None, "span"),
        ),
        check_vma=False,
    )
```

profile of v0, /device:TPU:14, one launch (start us, length us, event | category | flops | bytes accessed | tf_op | source)
XLA Modules:
  0.0 115.0 jit_solution(1528439476088058492)
XLA Ops:
  0.7 1.0 constant_dynamic-update-slice_fusion.1
  1.8 1.6 %collective-permute-start = (f32[8,4,16,1]{3,2,1,0:T(8,128)S(1)}, f32[8,4,16,1]{3,2,1,0:T(8,128)S(1)}, u32[]{:S(2)}, u32[]{:S(2)}) collective-permute-start(f32[8,4,16,1]{3,2,1,0:T(8,128)S(1)} %get-tuple-element.32), channel_id=1, source_target_pairs={{0,8},{8,16},{16,24},{24,0},{1,9},{9,17},{17,25},{25,1},{2,10},{10... | collective-permute-start | bytes 6152 | tf_op jit(solution)/shard_map/ppermute | solution.py:17
  3.4 0.4 collective-permute-start.1
  3.9 7.2 %collective-permute-done = f32[8,4,16,1]{3,2,1,0:T(8,128)S(1)} collective-permute-done((f32[8,4,16,1]{3,2,1,0:T(8,128)S(1)}, f32[8,4,16,1]{3,2,1,0:T(8,128)S(1)}, u32[]{:S(2)}, u32[]{:S(2)}) %collective-permute-start) | collective-permute-done | bytes 2080 | tf_op jit(solution)/shard_map/ppermute | solution.py:17
  11.0 5.3 %collective-permute-done.1 = f32[8,4,16,1]{3,2,1,0:T(8,128)S(1)} collective-permute-done((f32[8,4,16,1]{3,2,1,0:T(8,128)S(1)}, f32[8,4,16,1]{3,2,1,0:T(8,128)S(1)}, u32[]{:S(2)}, u32[]{:S(2)}) %collective-permute-start.1) | collective-permute-done | bytes 2080 | tf_op jit(solution)/shard_map/ppermute | solution.py:18
  16.4 0.3 pad_maximum_fusion.38
  16.6 1.3 %collective-permute-start.2 = (f32[8,4,1,130]{3,2,1,0:T(1,128)S(1)}, f32[8,4,1,130]{3,2,1,0:T(1,128)S(1)}, u32[]{:S(2)}, u32[]{:S(2)}) collective-permute-start(f32[8,4,1,130]{3,2,1,0:T(1,128)S(1)} %get-tuple-element.24), channel_id=1, source_target_pairs={{0,4},{1,5},{2,6},{3,7},{8,12},{9,13},{10,14},{11,15},{16,20},{17,... | collective-permute-start | bytes 49928 | tf_op jit(solution)/shard_map/ppermute | solution.py:17
  17.9 4.5 %collective-permute-start.3 = (f32[8,4,1,130]{3,2,1,0:T(1,128)S(1)}, f32[8,4,1,130]{3,2,1,0:T(1,128)S(1)}, u32[]{:S(2)}, u32[]{:S(2)}) collective-permute-start(f32[8,4,1,130]{3,2,1,0:T(1,128)S(1)} %get-tuple-element.25), channel_id=1, source_target_pairs={{4,0},{5,1},{6,2},{7,3},{12,8},{13,9},{14,10},{15,11},{20,16},{21,... | collective-permute-start | bytes 49928 | tf_op jit(solution)/shard_map/ppermute | solution.py:18
  22.5 1.5 %collective-permute-done.3 = f32[8,4,1,130]{3,2,1,0:T(1,128)S(1)} collective-permute-done((f32[8,4,1,130]{3,2,1,0:T(1,128)S(1)}, f32[8,4,1,130]{3,2,1,0:T(1,128)S(1)}, u32[]{:S(2)}, u32[]{:S(2)}) %collective-permute-start.3) | collective-permute-done | bytes 16672 | tf_op jit(solution)/shard_map/ppermute | solution.py:18
  24.1 0.2 pad_maximum_fusion.2
  24.3 1.9 %collective-permute-start.5 = (f32[8,1,18,130]{3,2,1,0:T(8,128)S(1)}, f32[8,1,18,130]{3,2,1,0:T(8,128)S(1)}, u32[]{:S(2)}, u32[]{:S(2)}) collective-permute-start(f32[8,1,18,130]{3,2,1,0:T(8,128)S(1)} %get-tuple-element.22), channel_id=1, source_target_pairs={{0,1},{1,2},{2,3},{4,5},{5,6},{6,7},{8,9},{9,10},{10,11},{12,13},{... | collective-permute-start | bytes 224648 | tf_op jit(solution)/shard_map/ppermute | solution.py:17
  26.2 3.6 %collective-permute-start.4 = (f32[8,1,18,130]{3,2,1,0:T(8,128)S(1)}, f32[8,1,18,130]{3,2,1,0:T(8,128)S(1)}, u32[]{:S(2)}, u32[]{:S(2)}) collective-permute-start(f32[8,1,18,130]{3,2,1,0:T(8,128)S(1)} %get-tuple-element.23), channel_id=1, source_target_pairs={{1,0},{2,1},{3,2},{5,4},{6,5},{7,6},{9,8},{10,9},{11,10},{13,12},{... | collective-permute-start | bytes 224648 | tf_op jit(solution)/shard_map/ppermute | solution.py:18
  29.9 1.4 %collective-permute-done.5 = f32[8,1,18,130]{3,2,1,0:T(8,128)S(1)} collective-permute-done((f32[8,1,18,130]{3,2,1,0:T(8,128)S(1)}, f32[8,1,18,130]{3,2,1,0:T(8,128)S(1)}, u32[]{:S(2)}, u32[]{:S(2)}) %collective-permute-start.5) | collective-permute-done | bytes 74912 | tf_op jit(solution)/shard_map/ppermute | solution.py:17
  31.3 1.8 %collective-permute-done.4 = f32[8,1,18,130]{3,2,1,0:T(8,128)S(1)} collective-permute-done((f32[8,1,18,130]{3,2,1,0:T(8,128)S(1)}, f32[8,1,18,130]{3,2,1,0:T(8,128)S(1)}, u32[]{:S(2)}, u32[]{:S(2)}) %collective-permute-start.4) | collective-permute-done | bytes 74912 | tf_op jit(solution)/shard_map/ppermute | solution.py:18
  33.5 0.7 copy-done.1
  34.3 0.5 fusion.14
  34.8 0.5 convolution_add_fusion.4
  35.2 0.3 fusion.21
  35.6 0.4 convolution_add_fusion.3
  36.0 0.5 convolution_add_fusion.2
  36.5 0.5 convolution_add_fusion.1
  37.0 0.4 copy-done.3
  37.4 0.6 fusion.2
  38.0 0.3 convolution_bitcast_fusion
  38.4 0.4 copy-done.2
  39.0 0.8 collective-permute-start.6
  39.8 1.3 %collective-permute-start.7 = (f32[4,4,16,3]{3,0,2,1:T(4,128)S(1)}, f32[4,4,16,3]{3,0,2,1:T(4,128)S(1)}, u32[]{:S(2)}, u32[]{:S(2)}) collective-permute-start(f32[4,4,16,3]{3,0,2,1:T(4,128)S(1)} %get-tuple-element.39), channel_id=1, source_target_pairs={{8,0},{16,8},{24,16},{0,24},{9,1},{17,9},{25,17},{1,25},{10,2},{18... | collective-permute-start | bytes 9224 | tf_op jit(solution)/shard_map/ppermute | solution.py:18
  41.1 2.9 %collective-permute-done.6 = f32[4,4,16,3]{3,0,2,1:T(4,128)S(1)} collective-permute-done((f32[4,4,16,3]{3,0,2,1:T(4,128)S(1)}, f32[4,4,16,3]{3,0,2,1:T(4,128)S(1)}, u32[]{:S(2)}, u32[]{:S(2)}) %collective-permute-start.6) | collective-permute-done | bytes 3104 | tf_op jit(solution)/shard_map/ppermute | solution.py:17
  44.0 2.1 %collective-permute-done.7 = f32[4,4,16,3]{3,0,2,1:T(4,128)S(1)} collective-permute-done((f32[4,4,16,3]{3,0,2,1:T(4,128)S(1)}, f32[4,4,16,3]{3,0,2,1:T(4,128)S(1)}, u32[]{:S(2)}, u32[]{:S(2)}) %collective-permute-start.7) | collective-permute-done | bytes 3104 | tf_op jit(solution)/shard_map/ppermute | solution.py:18
  46.4 1.3 %collective-permute-start.8 = (f32[4,4,3,134]{3,0,2,1:T(4,128)S(1)}, f32[4,4,3,134]{3,0,2,1:T(4,128)S(1)}, u32[]{:S(2)}, u32[]{:S(2)}) collective-permute-start(f32[4,4,3,134]{3,0,2,1:T(4,128)S(1)} %get-tuple-element.28), channel_id=1, source_target_pairs={{0,4},{1,5},{2,6},{3,7},{8,12},{9,13},{10,14},{11,15},{16,20},{17,... | collective-permute-start | bytes 77192 | tf_op jit(solution)/shard_map/ppermute | solution.py:17
  47.7 4.5 %collective-permute-start.9 = (f32[4,4,3,134]{3,0,2,1:T(4,128)S(1)}, f32[4,4,3,134]{3,0,2,1:T(4,128)S(1)}, u32[]{:S(2)}, u32[]{:S(2)}) collective-permute-start(f32[4,4,3,134]{3,0,2,1:T(4,128)S(1)} %get-tuple-element.29), channel_id=1, source_target_pairs={{4,0},{5,1},{6,2},{7,3},{12,8},{13,9},{14,10},{15,11},{20,16},{21,... | collective-permute-start | bytes 77192 | tf_op jit(solution)/shard_map/ppermute | solution.py:18
  52.4 1.6 %collective-permute-done.9 = f32[4,4,3,134]{3,0,2,1:T(4,128)S(1)} collective-permute-done((f32[4,4,3,134]{3,0,2,1:T(4,128)S(1)}, f32[4,4,3,134]{3,0,2,1:T(4,128)S(1)}, u32[]{:S(2)}, u32[]{:S(2)}) %collective-permute-start.9) | collective-permute-done | bytes 25760 | tf_op jit(solution)/shard_map/ppermute | solution.py:18
  54.0 0.4 pad_maximum_fusion.1
  54.4 1.9 %collective-permute-start.10 = (f32[4,3,22,134]{3,0,2,1:T(4,128)S(1)}, f32[4,3,22,134]{3,0,2,1:T(4,128)S(1)}, u32[]{:S(2)}, u32[]{:S(2)}) collective-permute-start(f32[4,3,22,134]{3,0,2,1:T(4,128)S(1)} %get-tuple-element.30), channel_id=1, source_target_pairs={{0,1},{1,2},{2,3},{4,5},{5,6},{6,7},{8,9},{9,10},{10,11},{12,13},{... | collective-permute-start | bytes 424520 | tf_op jit(solution)/shard_map/ppermute | solution.py:17
  56.4 3.8 %collective-permute-start.11 = (f32[4,3,22,134]{3,0,2,1:T(4,128)S(1)}, f32[4,3,22,134]{3,0,2,1:T(4,128)S(1)}, u32[]{:S(2)}, u32[]{:S(2)}) collective-permute-start(f32[4,3,22,134]{3,0,2,1:T(4,128)S(1)} %get-tuple-element.31), channel_id=1, source_target_pairs={{1,0},{2,1},{3,2},{5,4},{6,5},{7,6},{9,8},{10,9},{11,10},{13,12},{... | collective-permute-start | bytes 424520 | tf_op jit(solution)/shard_map/ppermute | solution.py:18
  60.2 0.7 copy.32
  60.9 1.3 %collective-permute-done.10 = f32[4,3,22,134]{3,0,2,1:T(4,128)S(1)} collective-permute-done((f32[4,3,22,134]{3,0,2,1:T(4,128)S(1)}, f32[4,3,22,134]{3,0,2,1:T(4,128)S(1)}, u32[]{:S(2)}, u32[]{:S(2)}) %collective-permute-start.10) | collective-permute-done | bytes 141536 | tf_op jit(solution)/shard_map/ppermute | solution.py:17
  62.2 1.8 %collective-permute-done.11 = f32[4,3,22,134]{3,0,2,1:T(4,128)S(1)} collective-permute-done((f32[4,3,22,134]{3,0,2,1:T(4,128)S(1)}, f32[4,3,22,134]{3,0,2,1:T(4,128)S(1)}, u32[]{:S(2)}, u32[]{:S(2)}) %collective-permute-start.11) | collective-permute-done | bytes 141536 | tf_op jit(solution)/shard_map/ppermute | solution.py:18
  64.0 0.5 pad_maximum_fusion
  64.5 0.3 multiply_add_fusion
  65.2 0.5 broadcast_multiply_fusion
  65.7 2.4 %broadcast_multiply_fusion.1 = (f32[3,8,20,132]{3,0,2,1:T(4,128)S(1)}, f32[3,8,20,132]{3,0,2,1:T(4,128)S(1)}) fusion(f32[8,20,132]{2,1,0:T(8,128)S(1)} %get-tuple-element.37, f32[3,10,22,134]{3,0,2,1:T(4,128)S(1)} %get-tuple-element.12, f32[8,20,132]{2,1,0:T(8,128)S(1)} %get-tuple-element.36, f32[4,10,22,134]{3,0,2,1:T(4,128)S(1)} %pad_maximum_fusion, ...), kind=kLoop, calls=%fused_computation.35 | loop fusion | flops 760320 | bytes 2703360 | tf_op jit(solution)/shard_map/mul | solution.py:57
  68.2 1.7 %broadcast_multiply_fusion.2 = (f32[3,6,18,130]{3,0,2,1:T(4,128)S(1)}, f32[3,6,18,130]{3,0,2,1:T(4,128)S(1)}) fusion(f32[6,18,130]{2,1,0:T(8,128)S(1)} %get-tuple-element.35, f32[3,8,20,132]{3,0,2,1:T(4,128)S(1)} %get-tuple-element.10, f32[6,18,130]{2,1,0:T(8,128)S(1)} %get-tuple-element.34, f32[4,10,22,134]{3,0,2,1:T(4,128)S(1)} %pad_maximum_fusion, ...), kind=kLoop, calls=%fused_computation.46 | loop fusion | flops 505440 | bytes 1797120 | tf_op jit(solution)/shard_map/mul | solution.py:57
  69.9 0.5 multiply_reduce_fusion
  70.5 0.5 convolution_bitcast_fusion.1
  71.0 42.7 %psum.7 = f32[3,512]{1,0:T(4,128)S(1)} all-reduce(f32[3,512]{1,0:T(4,128)S(1)} %convolution_bitcast_fusion.1), channel_id=1, replica_groups=mesh['circ'=4,'normal'=2,'span'=4] {'circ','normal','span'}, use_global_device_ids=true, to_apply=%region_1.0 | all-reduce | flops 1536 | bytes 12288 | tf_op jit(solution)/shard_map/psum | solution.py:105
  113.7 0.6 copy.33
  114.4 0.6 constant_dynamic-slice_fusion
  (35 shorter events, 1.9 us)
Async XLA Ops:
  0.6 37.4 %copy-start = (f32[3,5]{1,0:T(4,128)S(1)}, f32[3,5]{1,0:T(4,128)}, u32[]{:S(2)}) copy-start(f32[3,5]{1,0:T(4,128)} %param.14) | copy-start | bytes 184
  0.6 1.0 copy-start.4
  1.8 9.2 %collective-permute-start = (f32[8,4,16,1]{3,2,1,0:T(8,128)S(1)}, f32[8,4,16,1]{3,2,1,0:T(8,128)S(1)}, u32[]{:S(2)}, u32[]{:S(2)}) collective-permute-start(f32[8,4,16,1]{3,2,1,0:T(8,128)S(1)} %get-tuple-element.32), channel_id=1, source_target_pairs={{0,8},{8,16},{16,24},{24,0},{1,9},{9,17},{17,25},{25,1},{2,10},{10... | collective-permute-start | bytes 6152 | tf_op jit(solution)/shard_map/ppermute | solution.py:17
  3.4 12.9 %collective-permute-start.1 = (f32[8,4,16,1]{3,2,1,0:T(8,128)S(1)}, f32[8,4,16,1]{3,2,1,0:T(8,128)S(1)}, u32[]{:S(2)}, u32[]{:S(2)}) collective-permute-start(f32[8,4,16,1]{3,2,1,0:T(8,128)S(1)} %get-tuple-element.33), channel_id=1, source_target_pairs={{8,0},{16,8},{24,16},{0,24},{9,1},{17,9},{25,17},{1,25},{10,2},{18... | collective-permute-start | bytes 6152 | tf_op jit(solution)/shard_map/ppermute | solution.py:18
  3.9 18.6 %copy-start.6 = (f32[3,5,5]{2,0,1:T(4,128)S(1)}, f32[3,5,5]{2,0,1:T(4,128)}, u32[]{:S(2)}) copy-start(f32[3,5,5]{2,0,1:T(4,128)} %param.12) | copy-start | bytes 904
  16.6 5.9 %collective-permute-start.2 = (f32[8,4,1,130]{3,2,1,0:T(1,128)S(1)}, f32[8,4,1,130]{3,2,1,0:T(1,128)S(1)}, u32[]{:S(2)}, u32[]{:S(2)}) collective-permute-start(f32[8,4,1,130]{3,2,1,0:T(1,128)S(1)} %get-tuple-element.24), channel_id=1, source_target_pairs={{0,4},{1,5},{2,6},{3,7},{8,12},{9,13},{10,14},{11,15},{16,20},{17,... | collective-permute-start | bytes 49928 | tf_op jit(solution)/shard_map/ppermute | solution.py:17
  17.9 6.1 %collective-permute-start.3 = (f32[8,4,1,130]{3,2,1,0:T(1,128)S(1)}, f32[8,4,1,130]{3,2,1,0:T(1,128)S(1)}, u32[]{:S(2)}, u32[]{:S(2)}) collective-permute-start(f32[8,4,1,130]{3,2,1,0:T(1,128)S(1)} %get-tuple-element.25), channel_id=1, source_target_pairs={{4,0},{5,1},{6,2},{7,3},{12,8},{13,9},{14,10},{15,11},{20,16},{21,... | collective-permute-start | bytes 49928 | tf_op jit(solution)/shard_map/ppermute | solution.py:18
  22.5 7.4 %copy-start.7 = (f32[3,5,5]{2,0,1:T(4,128)S(1)}, f32[3,5,5]{2,0,1:T(4,128)}, u32[]{:S(2)}) copy-start(f32[3,5,5]{2,0,1:T(4,128)} %param.13) | copy-start | bytes 904
  24.3 7.0 %collective-permute-start.5 = (f32[8,1,18,130]{3,2,1,0:T(8,128)S(1)}, f32[8,1,18,130]{3,2,1,0:T(8,128)S(1)}, u32[]{:S(2)}, u32[]{:S(2)}) collective-permute-start(f32[8,1,18,130]{3,2,1,0:T(8,128)S(1)} %get-tuple-element.22), channel_id=1, source_target_pairs={{0,1},{1,2},{2,3},{4,5},{5,6},{6,7},{8,9},{9,10},{10,11},{12,13},{... | collective-permute-start | bytes 224648 | tf_op jit(solution)/shard_map/ppermute | solution.py:17
  26.2 6.8 %collective-permute-start.4 = (f32[8,1,18,130]{3,2,1,0:T(8,128)S(1)}, f32[8,1,18,130]{3,2,1,0:T(8,128)S(1)}, u32[]{:S(2)}, u32[]{:S(2)}) collective-permute-start(f32[8,1,18,130]{3,2,1,0:T(8,128)S(1)} %get-tuple-element.23), channel_id=1, source_target_pairs={{1,0},{2,1},{3,2},{5,4},{6,5},{7,6},{9,8},{10,9},{11,10},{13,12},{... | collective-permute-start | bytes 224648 | tf_op jit(solution)/shard_map/ppermute | solution.py:18
  33.2 0.9 copy-start.1
  36.5 0.9 copy-start.3
  38.0 0.8 copy-start.2
  39.0 5.0 %collective-permute-start.6 = (f32[4,4,16,3]{3,0,2,1:T(4,128)S(1)}, f32[4,4,16,3]{3,0,2,1:T(4,128)S(1)}, u32[]{:S(2)}, u32[]{:S(2)}) collective-permute-start(f32[4,4,16,3]{3,0,2,1:T(4,128)S(1)} %get-tuple-element.38), channel_id=1, source_target_pairs={{0,8},{8,16},{16,24},{24,0},{1,9},{9,17},{17,25},{25,1},{2,10},{10... | collective-permute-start | bytes 9224 | tf_op jit(solution)/shard_map/ppermute | solution.py:17
  39.8 6.4 %collective-permute-start.7 = (f32[4,4,16,3]{3,0,2,1:T(4,128)S(1)}, f32[4,4,16,3]{3,0,2,1:T(4,128)S(1)}, u32[]{:S(2)}, u32[]{:S(2)}) collective-permute-start(f32[4,4,16,3]{3,0,2,1:T(4,128)S(1)} %get-tuple-element.39), channel_id=1, source_target_pairs={{8,0},{16,8},{24,16},{0,24},{9,1},{17,9},{25,17},{1,25},{10,2},{18... | collective-permute-start | bytes 9224 | tf_op jit(solution)/shard_map/ppermute | solution.py:18
  46.4 6.0 %collective-permute-start.8 = (f32[4,4,3,134]{3,0,2,1:T(4,128)S(1)}, f32[4,4,3,134]{3,0,2,1:T(4,128)S(1)}, u32[]{:S(2)}, u32[]{:S(2)}) collective-permute-start(f32[4,4,3,134]{3,0,2,1:T(4,128)S(1)} %get-tuple-element.28), channel_id=1, source_target_pairs={{0,4},{1,5},{2,6},{3,7},{8,12},{9,13},{10,14},{11,15},{16,20},{17,... | collective-permute-start | bytes 77192 | tf_op jit(solution)/shard_map/ppermute | solution.py:17
  47.7 6.3 %collective-permute-start.9 = (f32[4,4,3,134]{3,0,2,1:T(4,128)S(1)}, f32[4,4,3,134]{3,0,2,1:T(4,128)S(1)}, u32[]{:S(2)}, u32[]{:S(2)}) collective-permute-start(f32[4,4,3,134]{3,0,2,1:T(4,128)S(1)} %get-tuple-element.29), channel_id=1, source_target_pairs={{4,0},{5,1},{6,2},{7,3},{12,8},{13,9},{14,10},{15,11},{20,16},{21,... | collective-permute-start | bytes 77192 | tf_op jit(solution)/shard_map/ppermute | solution.py:18
  54.4 7.8 %collective-permute-start.10 = (f32[4,3,22,134]{3,0,2,1:T(4,128)S(1)}, f32[4,3,22,134]{3,0,2,1:T(4,128)S(1)}, u32[]{:S(2)}, u32[]{:S(2)}) collective-permute-start(f32[4,3,22,134]{3,0,2,1:T(4,128)S(1)} %get-tuple-element.30), channel_id=1, source_target_pairs={{0,1},{1,2},{2,3},{4,5},{5,6},{6,7},{8,9},{9,10},{10,11},{12,13},{... | collective-permute-start | bytes 424520 | tf_op jit(solution)/shard_map/ppermute | solution.py:17
  56.4 7.6 %collective-permute-start.11 = (f32[4,3,22,134]{3,0,2,1:T(4,128)S(1)}, f32[4,3,22,134]{3,0,2,1:T(4,128)S(1)}, u32[]{:S(2)}, u32[]{:S(2)}) collective-permute-start(f32[4,3,22,134]{3,0,2,1:T(4,128)S(1)} %get-tuple-element.31), channel_id=1, source_target_pairs={{1,0},{2,1},{3,2},{5,4},{6,5},{7,6},{9,8},{10,9},{11,10},{13,12},{... | collective-permute-start | bytes 424520 | tf_op jit(solution)/shard_map/ppermute | solution.py:18
  68.2 1.7 %copy-start.5 = (f32[4,16,128]{2,1,0:T(8,128)S(1)}, f32[4,16,128]{2,1,0:T(8,128)}, u32[]{:S(2)}) copy-start(f32[4,16,128]{2,1,0:T(8,128)} %param.16) | copy-start | bytes 98308
  69.8 0.7 copy-start.8
where the time goes:
time: 115 us
  blocking collectives  42.7 us (37%)
  starting transfers between devices  27.1 us (24%)
  waiting for transfers between devices  27 us (23%)
  other arithmetic  8.29 us (7%)
  local copies, waits for them, and re-layouts  5.05 us (4%)
  matrix products  3.69 us (3%)
    psum x1, blocking collectives, on_device(): total = lax.psum(terms, ('circ', 'normal', 'span'))  42.7 us
    ppermute x6, starting transfers between devices, padded_2(): after = lax.ppermute(initial, axis, down)  18.3 us
    ppermute x6, waiting for transfers between devices, padded_2(): after = lax.ppermute(initial, axis, down)  14.1 us
    ppermute x6, waiting for transfers between devices, padded_2(): before = lax.ppermute(last, axis, up)  12.9 us
    ppermute x6, starting transfers between devices, padded_2(): before = lax.ppermute(last, axis, up)  8.85 us
    mul x3, other arithmetic, relax(): weighted = stiff_pad[None] * mesh_pad  4.64 us
    unnamed x22, local copies, waits for them, and re-layouts  4.09 us
  transfers between devices with their start and end apart: 12, of which 11 were waited for; matrix products, arithmetic and copies ran while one was open for 1% of the time, Pallas kernels for 0%

commit v1 on v0

--- a/solution.py
+++ b/solution.py
@@ -102,7 +102,8 @@
         panel_owner[:, :, None] == jnp.arange(panel_count, dtype=jnp.int32)[None, None, :]
     ).astype(jnp.float32)
     terms = jnp.einsum("mki,kip->mp", wall_sens, onehot, precision=lax.Precision.HIGHEST)
-    total = lax.psum(terms, ("circ", "normal", "span"))
+    parts = lax.all_gather(terms, ("circ", "normal", "span"), axis=0, tiled=False)
+    total = parts.sum(axis=0)
     panels = lax.dynamic_slice_in_dim(total, lax.axis_index("span") * PANEL_DEV, PANEL_DEV, 1)
     return (residual, mesh, panels)
 

time: 115 us -> 117 us (1.017)
  the two profiles are of different devices: /device:TPU:14 before, /device:TPU:0 now
where the time goes in v1:
time: 117 us; the launch traced here: 116 us
  blocking collectives  43.2 us (37%)
  waiting for transfers between devices  31.3 us (27%)
  starting transfers between devices  23.9 us (20%)
  other arithmetic  8.35 us (7%)
  local copies, waits for them, and re-layouts  4.9 us (4%)
  matrix products  3.7 us (3%)
    all_gather x1, blocking collectives, on_device(): lax.all_gather(terms, ('circ', 'normal', 'span'), axis=0, tiled=False)  43.2 us
    ppermute x6, waiting for transfers between devices, padded_2(): after = lax.ppermute(initial, axis, down)  20.4 us
    ppermute x6, starting transfers between devices, padded_2(): before = lax.ppermute(last, axis, up)  13.8 us
    ppermute x6, waiting for transfers between devices, padded_2(): before = lax.ppermute(last, axis, up)  10.9 us
    ppermute x6, starting transfers between devices, padded_2(): after = lax.ppermute(initial, axis, down)  10.1 us
    mul x3, other arithmetic, relax(): weighted = stiff_pad[None] * mesh_pad  4.64 us
    unnamed x22, local copies, waits for them, and re-layouts  3.93 us
  transfers between devices with their start and end apart: 12, of which 10 were waited for; matrix products, arithmetic and copies ran while one was open for 1% of the time, Pallas kernels for 0%

profile of v1, /device:TPU:0, one launch (start us, length us, event | category | flops | bytes accessed | tf_op | source)
XLA Modules:
  0.0 116.4 jit_solution(13396929754676314011)
XLA Ops:
  0.7 1.0 constant_dynamic-update-slice_fusion.1
  1.8 3.1 %collective-permute-start = (f32[8,4,16,1]{3,2,1,0:T(8,128)S(1)}, f32[8,4,16,1]{3,2,1,0:T(8,128)S(1)}, u32[]{:S(2)}, u32[]{:S(2)}) collective-permute-start(f32[8,4,16,1]{3,2,1,0:T(8,128)S(1)} %get-tuple-element.35), channel_id=1, source_target_pairs={{0,8},{8,16},{16,24},{24,0},{1,9},{9,17},{17,25},{25,1},{2,10},{10... | collective-permute-start | bytes 6152 | tf_op jit(solution)/shard_map/ppermute | solution.py:17
  4.9 2.1 %collective-permute-start.1 = (f32[8,4,16,1]{3,2,1,0:T(8,128)S(1)}, f32[8,4,16,1]{3,2,1,0:T(8,128)S(1)}, u32[]{:S(2)}, u32[]{:S(2)}) collective-permute-start(f32[8,4,16,1]{3,2,1,0:T(8,128)S(1)} %get-tuple-element.36), channel_id=1, source_target_pairs={{8,0},{16,8},{24,16},{0,24},{9,1},{17,9},{25,17},{1,25},{10,2},{18... | collective-permute-start | bytes 6152 | tf_op jit(solution)/shard_map/ppermute | solution.py:18
  7.0 7.1 %collective-permute-done = f32[8,4,16,1]{3,2,1,0:T(8,128)S(1)} collective-permute-done((f32[8,4,16,1]{3,2,1,0:T(8,128)S(1)}, f32[8,4,16,1]{3,2,1,0:T(8,128)S(1)}, u32[]{:S(2)}, u32[]{:S(2)}) %collective-permute-start) | collective-permute-done | bytes 2080 | tf_op jit(solution)/shard_map/ppermute | solution.py:17
  14.1 4.2 %collective-permute-done.1 = f32[8,4,16,1]{3,2,1,0:T(8,128)S(1)} collective-permute-done((f32[8,4,16,1]{3,2,1,0:T(8,128)S(1)}, f32[8,4,16,1]{3,2,1,0:T(8,128)S(1)}, u32[]{:S(2)}, u32[]{:S(2)}) %collective-permute-start.1) | collective-permute-done | bytes 2080 | tf_op jit(solution)/shard_map/ppermute | solution.py:18
  18.2 0.3 pad_maximum_fusion.38
  18.5 3.4 %collective-permute-start.2 = (f32[8,4,1,130]{3,2,1,0:T(1,128)S(1)}, f32[8,4,1,130]{3,2,1,0:T(1,128)S(1)}, u32[]{:S(2)}, u32[]{:S(2)}) collective-permute-start(f32[8,4,1,130]{3,2,1,0:T(1,128)S(1)} %get-tuple-element.27), channel_id=1, source_target_pairs={{0,4},{1,5},{2,6},{3,7},{8,12},{9,13},{10,14},{11,15},{16,20},{17,... | collective-permute-start | bytes 49928 | tf_op jit(solution)/shard_map/ppermute | solution.py:17
  22.0 1.3 %collective-permute-start.3 = (f32[8,4,1,130]{3,2,1,0:T(1,128)S(1)}, f32[8,4,1,130]{3,2,1,0:T(1,128)S(1)}, u32[]{:S(2)}, u32[]{:S(2)}) collective-permute-start(f32[8,4,1,130]{3,2,1,0:T(1,128)S(1)} %get-tuple-element.28), channel_id=1, source_target_pairs={{4,0},{5,1},{6,2},{7,3},{12,8},{13,9},{14,10},{15,11},{20,16},{21,... | collective-permute-start | bytes 49928 | tf_op jit(solution)/shard_map/ppermute | solution.py:18
  23.3 0.2 collective-permute-done.2
  23.5 4.2 %collective-permute-done.3 = f32[8,4,1,130]{3,2,1,0:T(1,128)S(1)} collective-permute-done((f32[8,4,1,130]{3,2,1,0:T(1,128)S(1)}, f32[8,4,1,130]{3,2,1,0:T(1,128)S(1)}, u32[]{:S(2)}, u32[]{:S(2)}) %collective-permute-start.3) | collective-permute-done | bytes 16672 | tf_op jit(solution)/shard_map/ppermute | solution.py:18
  27.8 0.2 pad_maximum_fusion.2
  28.0 1.3 %collective-permute-start.5 = (f32[8,1,18,130]{3,2,1,0:T(8,128)S(1)}, f32[8,1,18,130]{3,2,1,0:T(8,128)S(1)}, u32[]{:S(2)}, u32[]{:S(2)}) collective-permute-start(f32[8,1,18,130]{3,2,1,0:T(8,128)S(1)} %get-tuple-element.25), channel_id=1, source_target_pairs={{0,1},{1,2},{2,3},{4,5},{5,6},{6,7},{8,9},{9,10},{10,11},{12,13},{... | collective-permute-start | bytes 224648 | tf_op jit(solution)/shard_map/ppermute | solution.py:17
  29.3 1.3 %collective-permute-start.4 = (f32[8,1,18,130]{3,2,1,0:T(8,128)S(1)}, f32[8,1,18,130]{3,2,1,0:T(8,128)S(1)}, u32[]{:S(2)}, u32[]{:S(2)}) collective-permute-start(f32[8,1,18,130]{3,2,1,0:T(8,128)S(1)} %get-tuple-element.26), channel_id=1, source_target_pairs={{1,0},{2,1},{3,2},{5,4},{6,5},{7,6},{9,8},{10,9},{11,10},{13,12},{... | collective-permute-start | bytes 224648 | tf_op jit(solution)/shard_map/ppermute | solution.py:18
  30.6 3.7 %collective-permute-done.4 = f32[8,1,18,130]{3,2,1,0:T(8,128)S(1)} collective-permute-done((f32[8,1,18,130]{3,2,1,0:T(8,128)S(1)}, f32[8,1,18,130]{3,2,1,0:T(8,128)S(1)}, u32[]{:S(2)}, u32[]{:S(2)}) %collective-permute-start.4) | collective-permute-done | bytes 74912 | tf_op jit(solution)/shard_map/ppermute | solution.py:18
  34.8 0.7 copy-done.1
  35.6 0.5 fusion.14
  36.1 0.5 convolution_add_fusion.4
  36.6 0.3 fusion.21
  36.9 0.5 convolution_add_fusion.3
  37.4 0.5 convolution_add_fusion.2
  37.8 0.5 convolution_add_fusion.1
  38.3 0.4 copy-done.3
  38.7 0.6 fusion.2
  39.4 0.3 convolution_bitcast_fusion
  39.7 0.4 copy-done.2
  40.3 1.2 %collective-permute-start.6 = (f32[4,4,16,3]{3,0,2,1:T(4,128)S(1)}, f32[4,4,16,3]{3,0,2,1:T(4,128)S(1)}, u32[]{:S(2)}, u32[]{:S(2)}) collective-permute-start(f32[4,4,16,3]{3,0,2,1:T(4,128)S(1)} %get-tuple-element.41), channel_id=1, source_target_pairs={{0,8},{8,16},{16,24},{24,0},{1,9},{9,17},{17,25},{25,1},{2,10},{10... | collective-permute-start | bytes 9224 | tf_op jit(solution)/shard_map/ppermute | solution.py:17
  41.5 2.7 %collective-permute-start.7 = (f32[4,4,16,3]{3,0,2,1:T(4,128)S(1)}, f32[4,4,16,3]{3,0,2,1:T(4,128)S(1)}, u32[]{:S(2)}, u32[]{:S(2)}) collective-permute-start(f32[4,4,16,3]{3,0,2,1:T(4,128)S(1)} %get-tuple-element.42), channel_id=1, source_target_pairs={{8,0},{16,8},{24,16},{0,24},{9,1},{17,9},{25,17},{1,25},{10,2},{18... | collective-permute-start | bytes 9224 | tf_op jit(solution)/shard_map/ppermute | solution.py:18
  44.2 3.1 %collective-permute-done.6 = f32[4,4,16,3]{3,0,2,1:T(4,128)S(1)} collective-permute-done((f32[4,4,16,3]{3,0,2,1:T(4,128)S(1)}, f32[4,4,16,3]{3,0,2,1:T(4,128)S(1)}, u32[]{:S(2)}, u32[]{:S(2)}) %collective-permute-start.6) | collective-permute-done | bytes 3104 | tf_op jit(solution)/shard_map/ppermute | solution.py:17
  47.3 0.6 collective-permute-done.7
  48.1 1.6 %collective-permute-start.8 = (f32[4,4,3,134]{3,0,2,1:T(4,128)S(1)}, f32[4,4,3,134]{3,0,2,1:T(4,128)S(1)}, u32[]{:S(2)}, u32[]{:S(2)}) collective-permute-start(f32[4,4,3,134]{3,0,2,1:T(4,128)S(1)} %get-tuple-element.31), channel_id=1, source_target_pairs={{0,4},{1,5},{2,6},{3,7},{8,12},{9,13},{10,14},{11,15},{16,20},{17,... | collective-permute-start | bytes 77192 | tf_op jit(solution)/shard_map/ppermute | solution.py:17
  49.7 1.3 %collective-permute-start.9 = (f32[4,4,3,134]{3,0,2,1:T(4,128)S(1)}, f32[4,4,3,134]{3,0,2,1:T(4,128)S(1)}, u32[]{:S(2)}, u32[]{:S(2)}) collective-permute-start(f32[4,4,3,134]{3,0,2,1:T(4,128)S(1)} %get-tuple-element.32), channel_id=1, source_target_pairs={{4,0},{5,1},{6,2},{7,3},{12,8},{13,9},{14,10},{15,11},{20,16},{21,... | collective-permute-start | bytes 77192 | tf_op jit(solution)/shard_map/ppermute | solution.py:18
  51.0 0.4 collective-permute-done.8
  51.4 4.3 %collective-permute-done.9 = f32[4,4,3,134]{3,0,2,1:T(4,128)S(1)} collective-permute-done((f32[4,4,3,134]{3,0,2,1:T(4,128)S(1)}, f32[4,4,3,134]{3,0,2,1:T(4,128)S(1)}, u32[]{:S(2)}, u32[]{:S(2)}) %collective-permute-start.9) | collective-permute-done | bytes 25760 | tf_op jit(solution)/shard_map/ppermute | solution.py:18
  55.7 0.4 pad_maximum_fusion.1
  56.2 3.2 %collective-permute-start.10 = (f32[4,3,22,134]{3,0,2,1:T(4,128)S(1)}, f32[4,3,22,134]{3,0,2,1:T(4,128)S(1)}, u32[]{:S(2)}, u32[]{:S(2)}) collective-permute-start(f32[4,3,22,134]{3,0,2,1:T(4,128)S(1)} %get-tuple-element.33), channel_id=1, source_target_pairs={{0,1},{1,2},{2,3},{4,5},{5,6},{6,7},{8,9},{9,10},{10,11},{12,13},{... | collective-permute-start | bytes 424520 | tf_op jit(solution)/shard_map/ppermute | solution.py:17
  59.4 1.5 %collective-permute-start.11 = (f32[4,3,22,134]{3,0,2,1:T(4,128)S(1)}, f32[4,3,22,134]{3,0,2,1:T(4,128)S(1)}, u32[]{:S(2)}, u32[]{:S(2)}) collective-permute-start(f32[4,3,22,134]{3,0,2,1:T(4,128)S(1)} %get-tuple-element.34), channel_id=1, source_target_pairs={{1,0},{2,1},{3,2},{5,4},{6,5},{7,6},{9,8},{10,9},{11,10},{13,12},{... | collective-permute-start | bytes 424520 | tf_op jit(solution)/shard_map/ppermute | solution.py:18
  60.9 0.7 copy.54
  61.6 3.4 %collective-permute-done.11 = f32[4,3,22,134]{3,0,2,1:T(4,128)S(1)} collective-permute-done((f32[4,3,22,134]{3,0,2,1:T(4,128)S(1)}, f32[4,3,22,134]{3,0,2,1:T(4,128)S(1)}, u32[]{:S(2)}, u32[]{:S(2)}) %collective-permute-start.11) | collective-permute-done | bytes 141536 | tf_op jit(solution)/shard_map/ppermute | solution.py:18
  65.0 0.5 pad_maximum_fusion
  65.5 0.3 multiply_add_fusion
  66.2 0.5 broadcast_multiply_fusion
  66.8 2.4 %broadcast_multiply_fusion.1 = (f32[3,8,20,132]{3,0,2,1:T(4,128)S(1)}, f32[3,8,20,132]{3,0,2,1:T(4,128)S(1)}) fusion(f32[8,20,132]{2,1,0:T(8,128)S(1)} %get-tuple-element.40, f32[3,10,22,134]{3,0,2,1:T(4,128)S(1)} %get-tuple-element.15, f32[8,20,132]{2,1,0:T(8,128)S(1)} %get-tuple-element.39, f32[4,10,22,134]{3,0,2,1:T(4,128)S(1)} %pad_maximum_fusion, ...), kind=kLoop, calls=%fused_computation.35 | loop fusion | flops 760320 | bytes 2703360 | tf_op jit(solution)/shard_map/mul | solution.py:57
  69.2 1.7 %broadcast_multiply_fusion.2 = (f32[3,6,18,130]{3,0,2,1:T(4,128)S(1)}, f32[3,6,18,130]{3,0,2,1:T(4,128)S(1)}) fusion(f32[6,18,130]{2,1,0:T(8,128)S(1)} %get-tuple-element.38, f32[3,8,20,132]{3,0,2,1:T(4,128)S(1)} %get-tuple-element.13, f32[6,18,130]{2,1,0:T(8,128)S(1)} %get-tuple-element.37, f32[4,10,22,134]{3,0,2,1:T(4,128)S(1)} %pad_maximum_fusion, ...), kind=kLoop, calls=%fused_computation.46 | loop fusion | flops 505440 | bytes 1797120 | tf_op jit(solution)/shard_map/mul | solution.py:57
  70.9 0.5 multiply_reduce_fusion
  71.4 0.6 copy.55
  72.1 0.5 convolution_bitcast_fusion.1
  72.6 43.2 %all-gather.1 = f32[32,3,512]{2,1,0:T(4,128)S(1)} all-gather(f32[1,3,512]{2,1,0:T(4,128)S(1)} %convolution_bitcast_fusion.1), channel_id=2, replica_groups=mesh['circ'=4,'normal'=2,'span'=4] {'circ','normal','span'}, dimensions={0}, use_global_device_ids=true | all-gather | bytes 202752 | tf_op jit(solution)/shard_map/all_gather | solution.py:105
  115.8 0.6 constant_dynamic-slice_fusion
  (36 shorter events, 1.7 us)
Async XLA Ops:
  0.6 38.7 %copy-start = (f32[3,5]{1,0:T(4,128)S(1)}, f32[3,5]{1,0:T(4,128)}, u32[]{:S(2)}) copy-start(f32[3,5]{1,0:T(4,128)} %param.14) | copy-start | bytes 184
  0.6 1.0 copy-start.4
  1.8 12.3 %collective-permute-start = (f32[8,4,16,1]{3,2,1,0:T(8,128)S(1)}, f32[8,4,16,1]{3,2,1,0:T(8,128)S(1)}, u32[]{:S(2)}, u32[]{:S(2)}) collective-permute-start(f32[8,4,16,1]{3,2,1,0:T(8,128)S(1)} %get-tuple-element.35), channel_id=1, source_target_pairs={{0,8},{8,16},{16,24},{24,0},{1,9},{9,17},{17,25},{25,1},{2,10},{10... | collective-permute-start | bytes 6152 | tf_op jit(solution)/shard_map/ppermute | solution.py:17
  4.9 13.4 %collective-permute-start.1 = (f32[8,4,16,1]{3,2,1,0:T(8,128)S(1)}, f32[8,4,16,1]{3,2,1,0:T(8,128)S(1)}, u32[]{:S(2)}, u32[]{:S(2)}) collective-permute-start(f32[8,4,16,1]{3,2,1,0:T(8,128)S(1)} %get-tuple-element.36), channel_id=1, source_target_pairs={{8,0},{16,8},{24,16},{0,24},{9,1},{17,9},{25,17},{1,25},{10,2},{18... | collective-permute-start | bytes 6152 | tf_op jit(solution)/shard_map/ppermute | solution.py:18
  7.0 16.3 %copy-start.6 = (f32[3,5,5]{2,0,1:T(4,128)S(1)}, f32[3,5,5]{2,0,1:T(4,128)}, u32[]{:S(2)}) copy-start(f32[3,5,5]{2,0,1:T(4,128)} %param.12) | copy-start | bytes 904
  18.5 5.0 %collective-permute-start.2 = (f32[8,4,1,130]{3,2,1,0:T(1,128)S(1)}, f32[8,4,1,130]{3,2,1,0:T(1,128)S(1)}, u32[]{:S(2)}, u32[]{:S(2)}) collective-permute-start(f32[8,4,1,130]{3,2,1,0:T(1,128)S(1)} %get-tuple-element.27), channel_id=1, source_target_pairs={{0,4},{1,5},{2,6},{3,7},{8,12},{9,13},{10,14},{11,15},{16,20},{17,... | collective-permute-start | bytes 49928 | tf_op jit(solution)/shard_map/ppermute | solution.py:17
  22.0 5.8 %collective-permute-start.3 = (f32[8,4,1,130]{3,2,1,0:T(1,128)S(1)}, f32[8,4,1,130]{3,2,1,0:T(1,128)S(1)}, u32[]{:S(2)}, u32[]{:S(2)}) collective-permute-start(f32[8,4,1,130]{3,2,1,0:T(1,128)S(1)} %get-tuple-element.28), channel_id=1, source_target_pairs={{4,0},{5,1},{6,2},{7,3},{12,8},{13,9},{14,10},{15,11},{20,16},{21,... | collective-permute-start | bytes 49928 | tf_op jit(solution)/shard_map/ppermute | solution.py:18
  23.3 7.3 %copy-start.7 = (f32[3,5,5]{2,0,1:T(4,128)S(1)}, f32[3,5,5]{2,0,1:T(4,128)}, u32[]{:S(2)}) copy-start(f32[3,5,5]{2,0,1:T(4,128)} %param.13) | copy-start | bytes 904
  28.0 2.6 %collective-permute-start.5 = (f32[8,1,18,130]{3,2,1,0:T(8,128)S(1)}, f32[8,1,18,130]{3,2,1,0:T(8,128)S(1)}, u32[]{:S(2)}, u32[]{:S(2)}) collective-permute-start(f32[8,1,18,130]{3,2,1,0:T(8,128)S(1)} %get-tuple-element.25), channel_id=1, source_target_pairs={{0,1},{1,2},{2,3},{4,5},{5,6},{6,7},{8,9},{9,10},{10,11},{12,13},{... | collective-permute-start | bytes 224648 | tf_op jit(solution)/shard_map/ppermute | solution.py:17
  29.3 5.1 %collective-permute-start.4 = (f32[8,1,18,130]{3,2,1,0:T(8,128)S(1)}, f32[8,1,18,130]{3,2,1,0:T(8,128)S(1)}, u32[]{:S(2)}, u32[]{:S(2)}) collective-permute-start(f32[8,1,18,130]{3,2,1,0:T(8,128)S(1)} %get-tuple-element.26), channel_id=1, source_target_pairs={{1,0},{2,1},{3,2},{5,4},{6,5},{7,6},{9,8},{10,9},{11,10},{13,12},{... | collective-permute-start | bytes 224648 | tf_op jit(solution)/shard_map/ppermute | solution.py:18
  34.5 0.9 copy-start.1
  37.8 0.9 copy-start.3
  39.4 0.8 copy-start.2
  40.3 7.0 %collective-permute-start.6 = (f32[4,4,16,3]{3,0,2,1:T(4,128)S(1)}, f32[4,4,16,3]{3,0,2,1:T(4,128)S(1)}, u32[]{:S(2)}, u32[]{:S(2)}) collective-permute-start(f32[4,4,16,3]{3,0,2,1:T(4,128)S(1)} %get-tuple-element.41), channel_id=1, source_target_pairs={{0,8},{8,16},{16,24},{24,0},{1,9},{9,17},{17,25},{25,1},{2,10},{10... | collective-permute-start | bytes 9224 | tf_op jit(solution)/shard_map/ppermute | solution.py:17
  41.5 6.4 %collective-permute-start.7 = (f32[4,4,16,3]{3,0,2,1:T(4,128)S(1)}, f32[4,4,16,3]{3,0,2,1:T(4,128)S(1)}, u32[]{:S(2)}, u32[]{:S(2)}) collective-permute-start(f32[4,4,16,3]{3,0,2,1:T(4,128)S(1)} %get-tuple-element.42), channel_id=1, source_target_pairs={{8,0},{16,8},{24,16},{0,24},{9,1},{17,9},{25,17},{1,25},{10,2},{18... | collective-permute-start | bytes 9224 | tf_op jit(solution)/shard_map/ppermute | solution.py:18
  48.1 3.4 %collective-permute-start.8 = (f32[4,4,3,134]{3,0,2,1:T(4,128)S(1)}, f32[4,4,3,134]{3,0,2,1:T(4,128)S(1)}, u32[]{:S(2)}, u32[]{:S(2)}) collective-permute-start(f32[4,4,3,134]{3,0,2,1:T(4,128)S(1)} %get-tuple-element.31), channel_id=1, source_target_pairs={{0,4},{1,5},{2,6},{3,7},{8,12},{9,13},{10,14},{11,15},{16,20},{17,... | collective-permute-start | bytes 77192 | tf_op jit(solution)/shard_map/ppermute | solution.py:17
  49.7 6.0 %collective-permute-start.9 = (f32[4,4,3,134]{3,0,2,1:T(4,128)S(1)}, f32[4,4,3,134]{3,0,2,1:T(4,128)S(1)}, u32[]{:S(2)}, u32[]{:S(2)}) collective-permute-start(f32[4,4,3,134]{3,0,2,1:T(4,128)S(1)} %get-tuple-element.32), channel_id=1, source_target_pairs={{4,0},{5,1},{6,2},{7,3},{12,8},{13,9},{14,10},{15,11},{20,16},{21,... | collective-permute-start | bytes 77192 | tf_op jit(solution)/shard_map/ppermute | solution.py:18
  56.2 5.4 %collective-permute-start.10 = (f32[4,3,22,134]{3,0,2,1:T(4,128)S(1)}, f32[4,3,22,134]{3,0,2,1:T(4,128)S(1)}, u32[]{:S(2)}, u32[]{:S(2)}) collective-permute-start(f32[4,3,22,134]{3,0,2,1:T(4,128)S(1)} %get-tuple-element.33), channel_id=1, source_target_pairs={{0,1},{1,2},{2,3},{4,5},{5,6},{6,7},{8,9},{9,10},{10,11},{12,13},{... | collective-permute-start | bytes 424520 | tf_op jit(solution)/shard_map/ppermute | solution.py:17
  59.4 5.6 %collective-permute-start.11 = (f32[4,3,22,134]{3,0,2,1:T(4,128)S(1)}, f32[4,3,22,134]{3,0,2,1:T(4,128)S(1)}, u32[]{:S(2)}, u32[]{:S(2)}) collective-permute-start(f32[4,3,22,134]{3,0,2,1:T(4,128)S(1)} %get-tuple-element.34), channel_id=1, source_target_pairs={{1,0},{2,1},{3,2},{5,4},{6,5},{7,6},{9,8},{10,9},{11,10},{13,12},{... | collective-permute-start | bytes 424520 | tf_op jit(solution)/shard_map/ppermute | solution.py:18
  69.2 1.7 %copy-start.5 = (f32[4,16,128]{2,1,0:T(8,128)S(1)}, f32[4,16,128]{2,1,0:T(8,128)}, u32[]{:S(2)}) copy-start(f32[4,16,128]{2,1,0:T(8,128)} %param.16) | copy-start | bytes 98308
  71.4 0.7 copy-start.8
